TPU v7x, 512 devices: a whole 4x4x16 slice. The times are simulated.
512 devices in a mesh: grp: 4 (over y), seq: 32 (over z, core), mp: 4 (over x).
Axes of the slice: x: 4, y: 4, z: 16, core: 2. Of those that a mesh axis runs over, the one named last changes fastest.
Arguments:
- queries: bfloat16 [4, 4096, 2048], P('grp', 'seq', 'mp'), may hold values from -16 to 16
- d_out: bfloat16 [4, 4096, 2048], P('grp', 'seq', 'mp'), may hold values from -6 to 6
- neighbour_kv: bfloat16 [4, 256, 128, 2, 2048], P('grp', 'seq', None, None, 'mp'), may hold values from -16 to 16
- target: int32 [4, 256], P('grp', 'seq'), may hold values from -1 to 127, as said below
- bias: float32 [16, 191], P('mp'), may hold values from -6 to 6
Outputs:
- attended: bfloat16 [4, 4096, 2048], P('grp', 'seq', 'mp')
- d_query: bfloat16 [4, 4096, 2048], P('grp', 'seq', 'mp')
- d_kv: bfloat16 [4, 256, 128, 2, 2048], P('grp', 'seq', None, None, 'mp')
- d_bias: float32 [16, 191], P('mp')
Inputs may be any that keep to these rules, and one draw needn't show every extreme that they name: `target`: in each group every entry 0..127 stands in exactly one slot and -1 marks an empty slot. The slots of one index of seq hold at most 1 entries e with the same e // 4, and some index reaches that; some index of seq holds 8 entries.
All inputs are finite; a program needn't handle non-finite values.
Results may differ from a plain program's by a relative error of at most 0.011.
Values may be sent and summed in bfloat16 or wider, within the bound.
No kernel may reach another device: no remote copies, remote signals or barrier semaphores. Data moves between devices by JAX's collectives and lax.ppermute only.
A program may use at most 128 MiB of HBM per device.

v0:
```python
import jax
import jax.numpy as jnp
from jax import lax
from jax.sharding import PartitionSpec as P

STRETCH = 64
NB_LEN = 128
SEQ_LEN = 2048


def passed_along(block, axis, distance):
    devices = range(lax.axis_size(axis))
    route = [(i - distance, i) for i in devices if i - distance in devices]
    return lax.ppermute(block, axis, route)


def bias_grid(lookup, row_count, col_count):
    head_num = lookup.shape[0]
    span = row_count + col_count
    padded = jnp.pad(lookup, ((0, 0), (0, 1)))
    flattened = jnp.tile(padded, (1, row_count))
    flattened = jnp.pad(flattened, ((0, 0), (0, row_count)))
    shaped = flattened.reshape(head_num, row_count, span + 1)[:, :, :col_count]
    return shaped[:, :, ::-1]


def bias_fold(grads):
    head_num, row_count, col_count = grads.shape
    turned = grads[:, :, ::-1]
    padded = jnp.pad(turned, ((0, 0), (0, 0), (0, row_count)))
    flattened = padded.reshape(head_num, row_count * (row_count + col_count))
    flattened = flattened[:, : row_count * (row_count + col_count - 1)]
    return jnp.sum(flattened.reshape(head_num, row_count, row_count + col_count - 1), axis=1)


def take_rows(table, index, valid):
    rows = jnp.take(table, index, axis=0)
    shape = (valid.shape[0],) + (1,) * (rows.ndim - 1)
    return jnp.where(valid.reshape(shape), rows, jnp.zeros((), rows.dtype))


def exchange(block):
    return lax.all_to_all(block, "seq", split_axis=0, concat_axis=0, tiled=True)


def local(queries, d_out, neighbour_kv, target, bias):
    tok_rows = queries.shape[1]
    width_dev = queries.shape[2]
    head_count = bias.shape[0]
    head_depth = width_dev // head_count
    stretch_count = tok_rows // STRETCH
    per_owner = 2 * stretch_count
    shard_count = lax.axis_size("seq")
    my_index = lax.axis_index("seq")
    group_rows = tok_rows * shard_count
    seq_stretches = min(SEQ_LEN, group_rows) // STRETCH
    scale_factor = head_depth ** (-0.5)
    bias_rows = bias_grid(bias, STRETCH, NB_LEN).transpose(1, 0, 2)
    row_ids = jnp.arange(STRETCH)
    pair = jnp.stack([queries[0], d_out[0]], axis=1)
    pair_all = lax.all_gather(pair, "seq", axis=0, tiled=True)
    my_targets = target[0]
    slot_count = my_targets.shape[0]
    is_used = my_targets >= 0
    entry = jnp.where(is_used, my_targets, 0)
    stretch_of = entry // 2
    win_rows = stretch_of[:, None] * STRETCH + (STRETCH - 1) + row_ids[None, :]
    in_group = win_rows < group_rows
    win_rows = jnp.minimum(win_rows.reshape(-1), group_rows - 1)
    win = jnp.take(pair_all, win_rows, axis=0).reshape(slot_count, STRETCH, 2, width_dev)
    q_win = win[:, :, 0]
    g_win = win[:, :, 1]
    live_slot = (row_ids[None, :] == 0) | ((stretch_of[:, None] + 1) % seq_stretches != 0)
    q_keep = is_used[:, None] & in_group
    q_slots = jnp.where(q_keep[:, :, None], q_win, jnp.zeros((), q_win.dtype))
    g_slots = jnp.where((q_keep & live_slot)[:, :, None], g_win, jnp.zeros((), g_win.dtype))
    q_slots = q_slots.reshape(slot_count, STRETCH, head_count, head_depth)
    g_slots = g_slots.reshape(slot_count, STRETCH, head_count, head_depth)
    stored = neighbour_kv[0]
    key_rows = stored[:, :, 0].reshape(slot_count, NB_LEN, head_count, head_depth)
    value_rows = stored[:, :, 1].reshape(slot_count, NB_LEN, head_count, head_depth)
    scores = jnp.einsum("sihd,sjhd->sihj", q_slots, key_rows, preferred_element_type=jnp.float32)
    scores = scores * scale_factor + bias_rows[None]
    peak_val = jnp.max(scores, axis=-1)
    weights = jnp.exp(scores - peak_val[..., None])
    row_total = jnp.sum(weights, axis=-1)
    partial_value = jnp.einsum(
        "sihj,sjhd->sihd",
        weights.astype(jnp.bfloat16),
        value_rows,
        preferred_element_type=jnp.float32,
    )
    owner_of = jnp.where(is_used, my_targets // per_owner, -1)
    owner_match = owner_of[None, :] == jnp.arange(shard_count)[:, None]
    send_slot = jnp.argmax(owner_match, axis=1)
    send_has = jnp.any(owner_match, axis=1)
    part_send = take_rows(
        partial_value.astype(jnp.bfloat16).reshape(slot_count, STRETCH, width_dev),
        send_slot,
        send_has,
    )
    g_dot = jnp.einsum(
        "sihd,sihd->sih",
        g_slots.astype(jnp.float32),
        partial_value,
        precision=lax.Precision.HIGHEST,
    )
    mine = jnp.stack([peak_val, row_total, g_dot], axis=1)
    shared = jnp.concatenate(
        [
            mine.reshape(slot_count, -1),
            jnp.where(is_used, entry + 1, 0).astype(jnp.float32)[:, None],
        ],
        axis=1,
    )
    shared_wide = jnp.pad(shared, ((0, 0), (0, 1024 - shared.shape[1])))
    shared_all = lax.all_gather(shared_wide, "seq", tiled=True)[:, : shared.shape[1]]
    partner = entry + 1 - 2 * (entry % 2)
    partner_at = jnp.argmax(
        shared_all[None, :, -1] == (partner + 1).astype(jnp.float32)[:, None], axis=1
    )
    theirs = jnp.take(shared_all[:, :-1], partner_at, axis=0).reshape(mine.shape)
    both_peak = jnp.maximum(mine[:, 0], theirs[:, 0])
    mine_f = jnp.exp(mine[:, 0] - both_peak)
    theirs_f = jnp.exp(theirs[:, 0] - both_peak)
    both_total = mine_f * mine[:, 1] + theirs_f * theirs[:, 1]
    lse_slots = both_peak + jnp.log(both_total)
    dd_slots = (mine_f * mine[:, 2] + theirs_f * theirs[:, 2]) / both_total
    dd_slots = jnp.where(is_used[:, None, None], dd_slots, 0.0)
    part_recv = exchange(part_send)
    own_entries = my_index * per_owner + jnp.arange(per_owner)
    own_at = jnp.argmax(
        shared_all[None, :, -1] == (own_entries + 1).astype(jnp.float32)[:, None], axis=1
    )
    held_by = own_at // slot_count
    parts_own = jnp.take(part_recv, held_by, axis=0).astype(jnp.float32)
    parts_own = parts_own.reshape(stretch_count, 2, STRETCH, head_count, head_depth)
    stats_own = jnp.take(shared_all[:, :-1], own_at, axis=0).reshape(
        stretch_count, 2, 3, STRETCH, head_count
    )
    peaks_own = stats_own[:, :, 0]
    totals_own = stats_own[:, :, 1]
    stretch_ids = my_index * stretch_count + jnp.arange(stretch_count)
    is_live = (row_ids[None, :] == 0) | ((stretch_ids[:, None] + 1) % seq_stretches != 0)
    live_rows = is_live.astype(jnp.float32)
    top_peak = jnp.max(peaks_own, axis=1)
    factor = jnp.exp(peaks_own - top_peak[:, None])
    denominator = jnp.sum(factor * totals_own, axis=1)
    combined = jnp.sum(factor[..., None] * parts_own, axis=1) / denominator[..., None]
    combined = combined * live_rows[:, :, None, None]
    att_win = combined.astype(jnp.bfloat16).reshape(tok_rows, width_dev)
    att_before = passed_along(att_win[tok_rows - STRETCH :], "seq", 1)
    prob_full = jnp.exp(scores - lse_slots[..., None])
    prob_low = prob_full.astype(jnp.bfloat16)
    grad_prob = jnp.einsum(
        "sihd,sjhd->sihj", g_slots, value_rows, preferred_element_type=jnp.float32
    )
    grad_scores = prob_full * (grad_prob - dd_slots[..., None])
    scores_low = grad_scores.astype(jnp.bfloat16)
    grad_rows = (
        jnp.einsum("sihj,sjhd->sihd", scores_low, key_rows, preferred_element_type=jnp.float32)
        * scale_factor
    )
    mix_probs = jnp.stack([scores_low, prob_low], axis=1)
    mix_rows = jnp.stack([q_slots, g_slots], axis=1)
    grad_kv = jnp.einsum(
        "sxihj,sxihd->sjxhd", mix_probs, mix_rows, preferred_element_type=jnp.float32
    )
    kv_scale = jnp.array([scale_factor, 1.0], jnp.float32)[None, None, :, None, None]
    d_kv = (grad_kv * kv_scale).astype(jnp.bfloat16).reshape(slot_count, NB_LEN, 2, width_dev)
    bias_part = bias_fold(jnp.sum(grad_scores, axis=0).transpose(1, 0, 2))
    dq_rows = jnp.zeros((shard_count, stretch_count, STRETCH, width_dev), jnp.bfloat16)
    dq_owner = jnp.where(is_used, owner_of, shard_count)
    dq_rows = dq_rows.at[dq_owner, stretch_of % stretch_count].set(
        grad_rows.astype(jnp.bfloat16).reshape(slot_count, STRETCH, width_dev), mode="drop"
    )
    grad_win = lax.psum_scatter(dq_rows, "seq", scatter_dimension=0, tiled=True)
    grad_win = grad_win.reshape(tok_rows, width_dev)
    grad_before = passed_along(grad_win[tok_rows - STRETCH :], "seq", 1)
    attended = jnp.concatenate([att_before[1:], att_win[: tok_rows - STRETCH + 1]])
    d_query = jnp.concatenate([grad_before[1:], grad_win[: tok_rows - STRETCH + 1]])
    raw_sum = lax.psum(lax.psum(bias_part, "seq"), "grp")
    squares = lax.psum(jnp.sum(raw_sum * raw_sum), "mp")
    d_bias = raw_sum * jnp.minimum(1.0, 1.0 / jnp.sqrt(squares + 1e-12))
    return (attended[None], d_query[None], d_kv[None], d_bias)


def solution(mesh):
    in_specs = (
        P("grp", "seq", "mp"),
        P("grp", "seq", "mp"),
        P("grp", "seq", None, None, "mp"),
        P("grp", "seq"),
        P("mp", None),
    )
    out_specs = (
        P("grp", "seq", "mp"),
        P("grp", "seq", "mp"),
        P("grp", "seq", None, None, "mp"),
        P("mp", None),
    )
    return jax.shard_map(local, mesh=mesh, in_specs=in_specs, out_specs=out_specs, check_vma=False)
```

profile of v0, /device:TPU:1, one launch (start us, length us, event | category | flops | bytes accessed | tf_op | source)
XLA Modules:
  0.0 341.9 jit_solution(12824938684409181369)
XLA Ops:
  7.2 1.1 pad_maximum_fusion.1
  8.4 1.0 copy.104
  9.4 0.7 fusion.44
  10.3 0.7 copy.111
  11.0 0.7 pad.16
  12.3 3.8 %copy.106 = bf16[1,8,128,2,512]{2,4,1,3,0:T(8,128)(2,1)} copy(bf16[1,8,128,2,512]{4,3,2,1,0:T(2,128)(2,1)S(1)} %copy-done.8) | data formatting | bytes 4194304 | tf_op args[2]
  16.3 0.7 fusion.33
  16.9 2.8 fusion.54
  19.7 75.7 %all-gather.3.cloned.1.call-done = bf16[4096,2,512]{2,1,0:T(2,128)(2,1)} async-done(((bf16[128,2,512]{2,1,0:T(2,128)(2,1)}), bf16[4096,2,512]{2,1,0:T(2,128)(2,1)}) %all-gather.3.cloned.1.call-update) | async-done | bytes 8388624 | tf_op jit(solution)/shard_map/all_gather | solution.py:61
  95.4 6.4 %gather_fusion = bf16[512,2,512]{2,1,0:T(2,128)(2,1)S(1)} fusion(bf16[4096,2,512]{2,1,0:T(2,128)(2,1)} %all-gather.3.cloned.1.call-done, s32[1024]{0:T(1024)S(1)} %pad_clamp_fusion.4), kind=kCustom, calls=%fused_computation | custom fusion | bytes 2099200 | tf_op jit(solution)/shard_map/jit(_take)/gather | solution.py:70
  102.4 0.7 broadcast_select_fusion.1
  103.1 1.4 fusion.53
  104.6 0.5 fusion.57
  105.1 2.0 multiply_reduce_fusion
  107.5 0.6 select_maximum_fusion
  108.2 0.6 iota_reduce_fusion.1
  108.9 1.1 copy.160
  110.1 2.0 gather_fusion.2
  112.1 3.3 select_select_fusion
  115.3 7.8 %all-to-all-start = ((bf16[32,64,512]{2,1,0:T(8,128)(2,1)}), bf16[32,64,512]{2,1,0:T(8,128)(2,1)}, u32[]{:S(2)}, u32[]{:S(2)}) async-start(bf16[32,64,512]{2,1,0:T(8,128)(2,1)} %select_select_fusion), calls=%async_computation | async-start | bytes 4194304 | tf_op jit(solution)/shard_map/all_to_all | solution.py:43
  123.2 76.4 %all-gather.5.cloned.1.call-done = f32[256,1024]{1,0:T(8,128)} async-done(((f32[8,1024]{1,0:T(8,128)}), f32[256,1024]{1,0:T(8,128)}) %all-gather.5.cloned.1.call-update) | async-done | bytes 1048592 | tf_op jit(solution)/shard_map/all_gather | solution.py:117
  199.6 1.0 slice_reduce_fusion
  200.6 0.7 iota_reduce_fusion
  201.3 0.5 compare_and_fusion.1
  201.9 2.1 slice.108
  203.9 2.3 gather_fusion.4
  206.2 0.9 copy.120
  207.2 0.8 copy.121
  207.9 1.0 broadcast_select_fusion.3
  208.9 0.8 log_add_fusion
  209.7 0.8 fusion.3
  210.5 1.0 copy-done
  211.5 0.8 fusion.5
  212.4 2.4 broadcast_in_dim.169
  214.9 2.5 scatter_fusion
  217.4 0.6 copy-done.24
  218.4 0.9 squeeze.45
  219.3 1.0 squeeze.44
  220.3 1.0 fusion.55
  222.0 45.5 %psum.21 = f32[4,191]{1,0:T(4,128)S(1)} all-reduce(f32[4,191]{1,0:T(4,128)S(1)} %reduce_sum.58), channel_id=1, replica_groups=mesh['grp'=4,'seq'=32,'mp'=4] {'seq'}, use_global_device_ids=true, to_apply=%region_13.14 | all-reduce | flops 764 | bytes 6112 | tf_op jit(solution)/shard_map/psum | solution.py:182
  267.5 8.4 %psum.22 = f32[4,191]{1,0:T(4,128)S(1)} all-reduce(f32[4,191]{1,0:T(4,128)S(1)} %psum.21), channel_id=1, replica_groups=mesh['grp'=4,'seq'=32,'mp'=4] {'grp'}, use_global_device_ids=true, to_apply=%region_14.15 | all-reduce | flops 764 | bytes 6112 | tf_op jit(solution)/shard_map/psum | solution.py:182
  275.9 0.6 multiply_reduce_fusion.2
  276.5 1.2 copy_select_fusion.1
  277.7 10.2 %psum.23 = f32[]{:T(128)} all-reduce(f32[]{:T(128)} %multiply_reduce_fusion.2), channel_id=1, replica_groups=mesh['grp'=4,'seq'=32,'mp'=4] {'mp'}, use_global_device_ids=true, to_apply=%region_16.17 | all-reduce | flops 1 | bytes 8 | tf_op jit(solution)/shard_map/psum | solution.py:183
  287.9 0.7 iota_reduce_fusion.2
  288.6 0.6 broadcast_in_dim.159
  289.2 0.6 broadcast_in_dim.155
  289.9 1.7 gather_fusion.1
  292.2 0.4 gather.31
  292.7 0.3 fusion.13
  293.0 2.2 multiply_convert_fusion
  295.2 3.8 %copy.129 = bf16[1,8,128,2,512]{4,3,2,1,0:T(2,128)(2,1)} copy(bf16[1,8,128,2,512]{2,4,3,1,0:T(8,128)(2,1)S(1)} %bitcast.165) | data formatting | bytes 4194304
  299.2 0.6 broadcast_multiply_fusion
  299.8 2.2 gather_fusion.3
  302.1 0.5 multiply_reduce_fusion.1
  302.9 5.1 %collective-permute-start = (bf16[64,512]{1,0:T(8,128)(2,1)S(1)}, bf16[64,512]{1,0:T(8,128)(2,1)S(1)}, u32[]{:S(2)}, u32[]{:S(2)}) collective-permute-start(bf16[64,512]{1,0:T(8,128)(2,1)S(1)} %bitcast.180), channel_id=1, source_target_pairs={{0,4},{4,8},{8,12},{12,16},{16,20},{20,24},{24,28},{28,32},{32,36}... | collective-permute-start | bytes 196616 | tf_op jit(solution)/shard_map/ppermute | solution.py:14
  308.2 1.9 collective-permute-done
  310.1 18.2 %reduce-scatter.2.cloned.1.call-done = bf16[1,2,64,512]{3,2,1,0:T(8,128)(2,1)} async-done(((bf16[32,2,64,512]{3,2,1,0:T(8,128)(2,1)}), bf16[1,2,64,512]{3,2,1,0:T(8,128)(2,1)}) %reduce-scatter.2.cloned.1.call-update) | async-done | bytes 131088 | tf_op jit(solution)/shard_map/reduce_scatter | solution.py:177
  328.3 0.8 slice_bitcast_fusion.1
  329.1 3.4 collective-permute-start.1
  332.6 0.7 maximum_bitcast_fusion
  333.2 0.9 slice.121
  334.1 0.5 collective-permute-done.1
  334.7 0.7 maximum_bitcast_fusion.1
  (117 shorter events, 3.9 us)
Async XLA Ops:
  7.2 5.2 %copy-start.8 = (bf16[1,8,128,2,512]{4,3,2,1,0:T(2,128)(2,1)S(1)}, bf16[1,8,128,2,512]{4,3,2,1,0:T(2,128)(2,1)}, u32[]{:S(2)}) copy-start(bf16[1,8,128,2,512]{4,3,2,1,0:T(2,128)(2,1)} %param.8) | copy-start | bytes 6291460
  7.2 88.3 %all-gather.3.cloned.1.call-start = ((), (), s32[]{:S(2)}) async-start(), calls=%async_computation.2 | async-start | bytes 8650752 | tf_op jit(solution)/shard_map/all_gather | solution.py:61
  9.4 190.3 %all-gather.5.cloned.1.call-start = ((), (), s32[]{:S(2)}) async-start(), calls=%async_computation.3 | async-start | bytes 1081344 | tf_op jit(solution)/shard_map/all_gather | solution.py:117
  10.1 6.1 %copy-start.21 = (pred[8]{0:T(512)(128)(4,1)}, pred[8]{0:T(512)(128)(4,1)S(1)}, u32[]{:S(2)}) copy-start(pred[8]{0:T(512)(128)(4,1)S(1)} %get-tuple-element.54) | copy-start | bytes 28
  16.1 3.6 %copy-start.23 = (pred[64]{0:T(512)(128)(4,1)}, pred[64]{0:T(512)(128)(4,1)S(1)}, u32[]{:S(2)}) copy-start(pred[64]{0:T(512)(128)(4,1)S(1)} %iota_compare_fusion.2) | copy-start | bytes 196
  16.2 86.1 %copy-start.17 = (pred[8,64]{1,0:T(8,128)(4,1)}, pred[8,64]{1,0:T(8,128)(4,1)S(1)}, u32[]{:S(2)}) copy-start(pred[8,64]{1,0:T(8,128)(4,1)S(1)} %get-tuple-element.51) | copy-start | bytes 1540
  16.2 86.9 %copy-start.15 = (pred[8,64]{1,0:T(8,128)(4,1)}, pred[8,64]{1,0:T(8,128)(4,1)S(1)}, u32[]{:S(2)}) copy-start(pred[8,64]{1,0:T(8,128)(4,1)S(1)} %get-tuple-element.50) | copy-start | bytes 1540
  102.1 2.5 copy-start.4
  102.4 2.2 copy-start.2
  105.1 3.1 copy-start.22
  107.1 1.8 copy-start.12
  107.1 1.8 copy-start.13
  115.3 184.5 %all-to-all-start = ((bf16[32,64,512]{2,1,0:T(8,128)(2,1)}), bf16[32,64,512]{2,1,0:T(8,128)(2,1)}, u32[]{:S(2)}, u32[]{:S(2)}) async-start(bf16[32,64,512]{2,1,0:T(8,128)(2,1)} %select_select_fusion), calls=%async_computation | async-start | bytes 4194304 | tf_op jit(solution)/shard_map/all_to_all | solution.py:43
  123.2 86.5 %copy-start.9 = (bf16[8,64,4,128]{3,2,1,0:T(4,128)(2,1)S(1)}, bf16[8,64,4,128]{3,2,1,0:T(4,128)(2,1)}, u32[]{:S(2)}) copy-start(bf16[8,64,4,128]{3,2,1,0:T(4,128)(2,1)} %get-tuple-element.35) | copy-start | bytes 1572868
  123.2 205.1 %reduce-scatter.2.cloned.1.call-start = ((), (), s32[]{:S(2)}) async-start(), calls=%async_computation.4 | async-start | bytes 4325376 | tf_op jit(solution)/shard_map/reduce_scatter | solution.py:177
  200.6 3.3 copy-start.19
  207.9 3.5 %copy-start.3 = (bf16[8,128,1,512]{1,3,0,2:T(8,128)(2,1)S(1)}, bf16[8,128,1,512]{1,3,0,2:T(8,128)(2,1)}, u32[]{:S(2)}) copy-start(bf16[8,128,1,512]{1,3,0,2:T(8,128)(2,1)} %get-tuple-element.38) | copy-start | bytes 3145732
  209.7 2.6 copy-start.10
  210.5 1.0 copy-start
  212.4 2.4 copy-start.14
  217.4 0.7 copy-start.24
  217.4 1.0 copy-start.5
  217.4 3.0 copy-start.1
  219.3 57.2 %copy-start.6 = (bf16[8,1,64,4,128]{4,3,2,0,1:T(4,128)(2,1)S(1)}, bf16[8,1,64,4,128]{4,3,2,0,1:T(4,128)(2,1)}, u32[]{:S(2)}) copy-start(bf16[8,1,64,4,128]{4,3,2,0,1:T(4,128)(2,1)} %squeeze.45) | copy-start | bytes 1572868
  219.3 57.2 %copy-start.16 = (pred[8,64]{1,0:T(8,128)(4,1)S(1)}, pred[8,64]{1,0:T(8,128)(4,1)}, u32[]{:S(2)}) copy-start(pred[8,64]{1,0:T(8,128)(4,1)} %copy-done.15) | copy-start | bytes 1540
  219.3 57.2 %copy-start.18 = (pred[8,64]{1,0:T(8,128)(4,1)S(1)}, pred[8,64]{1,0:T(8,128)(4,1)}, u32[]{:S(2)}) copy-start(pred[8,64]{1,0:T(8,128)(4,1)} %copy-done.17) | copy-start | bytes 1540
  220.3 56.2 %copy-start.7 = (bf16[8,1,64,4,128]{4,3,2,0,1:T(4,128)(2,1)S(1)}, bf16[8,1,64,4,128]{4,3,2,0,1:T(4,128)(2,1)}, u32[]{:S(2)}) copy-start(bf16[8,1,64,4,128]{4,3,2,0,1:T(4,128)(2,1)} %squeeze.44) | copy-start | bytes 1572868
  221.3 66.6 %copy-start.20 = (f32[256]{0:T(256)S(1)}, f32[256]{0:T(256)}, u32[]{:S(2)}) copy-start(f32[256]{0:T(256)} %copy-done.19) | copy-start | bytes 3076
  221.4 71.2 %copy-start.11 = (f32[8,64,4]{1,2,0:T(4,128)S(1)}, f32[8,64,4]{1,2,0:T(4,128)}, u32[]{:S(2)}) copy-start(f32[8,64,4]{1,2,0:T(4,128)} %copy-done.10) | copy-start | bytes 24580
  295.2 3.8 %copy-start.26 = (pred[2,2]{1,0:T(4,128)(4,1)S(1)}, pred[2,2]{1,0:T(4,128)(4,1)}, u32[]{:S(2)}) copy-start(pred[2,2]{1,0:T(4,128)(4,1)} %broadcast_in_dim.155) | copy-start | bytes 16
  299.0 3.0 copy-start.25
  302.9 7.1 %collective-permute-start = (bf16[64,512]{1,0:T(8,128)(2,1)S(1)}, bf16[64,512]{1,0:T(8,128)(2,1)S(1)}, u32[]{:S(2)}, u32[]{:S(2)}) collective-permute-start(bf16[64,512]{1,0:T(8,128)(2,1)S(1)} %bitcast.180), channel_id=1, source_target_pairs={{0,4},{4,8},{8,12},{12,16},{16,20},{20,24},{24,28},{28,32},{32,36}... | collective-permute-start | bytes 196616 | tf_op jit(solution)/shard_map/ppermute | solution.py:14
  329.1 5.5 %collective-permute-start.1 = (bf16[64,512]{1,0:T(8,128)(2,1)S(1)}, bf16[64,512]{1,0:T(8,128)(2,1)S(1)}, u32[]{:S(2)}, u32[]{:S(2)}) collective-permute-start(bf16[64,512]{1,0:T(8,128)(2,1)S(1)} %slice_bitcast_fusion.1), channel_id=1, source_target_pairs={{0,4},{4,8},{8,12},{12,16},{16,20},{20,24},{24,28},{28,32},{32,36}... | collective-permute-start | bytes 196616 | tf_op jit(solution)/shard_map/ppermute | solution.py:14
Sparse Core Ops, SparseCore 0:
  10.1 85.2 all-gather.2
  108.3 91.2 all-gather.4
  217.5 110.7 reduce-scatter.1
where the time goes:
time: 343 us; the launch traced here: 342 us
  waiting for transfers between devices  173 us (50%)
  blocking collectives  64.2 us (19%)
  local copies, waits for them, and re-layouts  47.5 us (14%)
  other arithmetic  19.6 us (6%)
  starting transfers between devices  16.5 us (5%)
  between operations  15 us (4%)
  matrix products  6.32 us (2%)
    all_gather x1, waiting for transfers between devices, local(): lax.all_gather(shared_wide, 'seq', tiled=True)[:, :shared.shape[1]]  76.4 us
    all_gather x1, waiting for transfers between devices, local(): pair_all = lax.all_gather(pair, 'seq', axis=0, tiled=True)  75.7 us
    psum x2, blocking collectives, local(): raw_sum = lax.psum(lax.psum(bias_part, 'seq'), 'grp')  53.9 us
    reduce_scatter x1, waiting for transfers between devices, local(): grad_win = lax.psum_scatter(dq_rows, 'seq', scatter_dimension=0, tiled=True)  18.2 us
    psum x1, blocking collectives, local(): squares = lax.psum(jnp.sum(raw_sum * raw_sum), 'mp')  10.2 us
    unnamed x58, local copies, waits for them, and re-layouts  9.33 us
    ppermute x2, starting transfers between devices, passed_along(): return lax.ppermute(block, axis, route)  8.55 us
    all_to_all x1, starting transfers between devices, exchange(): return lax.all_to_all(block, 'seq', split_axis=0, concat_axis=0, tiled=True)  7.84 us
  transfers between devices with their start and end apart: 6, of which 5 were waited for; matrix products, arithmetic and copies ran while one was open for 16% of the time, Pallas kernels for 0%

commit v1 on v0

--- a/solution.py
+++ b/solution.py
@@ -58,7 +58,9 @@
     bias_rows = bias_grid(bias, STRETCH, NB_LEN).transpose(1, 0, 2)
     row_ids = jnp.arange(STRETCH)
     pair = jnp.stack([queries[0], d_out[0]], axis=1)
-    pair_all = lax.all_gather(pair, "seq", axis=0, tiled=True)
+    pair_all = jnp.concatenate(
+        lax.all_to_all(jnp.stack([pair] * lax.axis_size("seq")), "seq", 0, 0), axis=0
+    )
     my_targets = target[0]
     slot_count = my_targets.shape[0]
     is_used = my_targets >= 0

time: 343 us -> 649 us (1.89)
  waiting for transfers between devices: 173 us -> 450 us
  starting transfers between devices: 16.5 us -> 39.2 us
  local copies, waits for them, and re-layouts: 47.5 us -> 54.7 us
    all_to_all x0 -> x1, waiting for transfers between devices: none -> 352 us  [local(): lax.all_to_all(jnp.stack([pair] * lax.axis_size('seq')), 'seq', 0, 0)]
    all_gather x1 -> x0, waiting for transfers between devices: 75.7 us -> none  [local(): pair_all = lax.all_gather(pair, 'seq', axis=0, tiled=True)]
    all_to_all x0 -> x1, starting transfers between devices: none -> 16.9 us  [local(): lax.all_to_all(jnp.stack([pair] * lax.axis_size('seq')), 'seq', 0, 0)]
    another operation x0 -> x1, local copies, waits for them, and re-layouts: none -> 8.68 us  [local(): jnp.stack([pair] * lax.axis_size('seq'))]
  transfers between devices with their start and end apart: 6 -> 6, of which waited for: 5 -> 5; matrix products, arithmetic and copies ran while one was open for 16% -> 8% of each run, Pallas kernels for 0% -> 0%
where the time goes in v1:
time: 649 us; the launch traced here: 648 us
  waiting for transfers between devices  450 us (69%)
  blocking collectives  63.6 us (10%)
  local copies, waits for them, and re-layouts  54.7 us (8%)
  starting transfers between devices  39.2 us (6%)
  other arithmetic  18.8 us (3%)
  between operations  15.3 us (2%)
    all_to_all x1, waiting for transfers between devices, local(): lax.all_to_all(jnp.stack([pair] * lax.axis_size('seq')), 'seq', 0, 0)  352 us
    all_gather x1, waiting for transfers between devices, local(): lax.all_gather(shared_wide, 'seq', tiled=True)[:, :shared.shape[1]]  77.9 us
    psum x2, blocking collectives, local(): raw_sum = lax.psum(lax.psum(bias_part, 'seq'), 'grp')  54.5 us
    reduce_scatter x1, waiting for transfers between devices, local(): grad_win = lax.psum_scatter(dq_rows, 'seq', scatter_dimension=0, tiled=True)  17.8 us
    all_to_all x1, starting transfers between devices, local(): lax.all_to_all(jnp.stack([pair] * lax.axis_size('seq')), 'seq', 0, 0)  16.9 us
  transfers between devices with their start and end apart: 6, of which 5 were waited for; matrix products, arithmetic and copies ran while one was open for 8% of the time, Pallas kernels for 0%

profile of v1, /device:TPU:1, one launch (start us, length us, event | category | flops | bytes accessed | tf_op | source)
XLA Modules:
  0.0 647.8 jit_solution(11398642001018481064)
XLA Ops:
  7.2 1.0 pad_maximum_fusion.1
  8.4 8.7 %stack.21 = bf16[32,128,2,512]{3,2,1,0:T(2,128)(2,1)} broadcast(bf16[128,2,512]{2,1,0:T(2,128)(2,1)S(1)} %copy.104), dimensions={1,2,3} | broadcast | bytes 8650752 | tf_op jit(solution)/shard_map/stack | solution.py:62
  17.1 16.9 %all-to-all-start = ((bf16[32,128,2,512]{3,2,1,0:T(2,128)(2,1)}), bf16[32,128,2,512]{3,2,1,0:T(2,128)(2,1)}, u32[]{:S(2)}, u32[]{:S(2)}) async-start(bf16[32,128,2,512]{3,2,1,0:T(2,128)(2,1)} %stack.21), calls=%async_computation | async-start | bytes 16777216 | tf_op jit(solution)/shard_map/all_to_all | solution.py:62
  35.0 0.7 copy-done.8
  35.7 3.8 copy.106
  39.7 0.7 fusion.33
  40.3 2.7 fusion.54
  43.0 351.6 %all-to-all-done = bf16[32,128,2,512]{3,2,1,0:T(2,128)(2,1)} async-done(((bf16[32,128,2,512]{3,2,1,0:T(2,128)(2,1)}), bf16[32,128,2,512]{3,2,1,0:T(2,128)(2,1)}, u32[]{:S(2)}, u32[]{:S(2)}) %all-to-all-start) | async-done | bytes 8388640 | tf_op jit(solution)/shard_map/all_to_all | solution.py:62
  394.7 6.4 gather_fusion
  401.6 1.4 fusion.53
  403.1 0.7 broadcast_select_fusion.1
  403.8 0.5 fusion.57
  404.3 2.0 multiply_reduce_fusion
  406.7 0.6 select_maximum_fusion
  407.4 0.6 iota_reduce_fusion.1
  408.1 1.1 copy.160
  409.3 2.0 gather_fusion.2
  411.3 3.3 select_select_fusion
  414.5 12.9 %all-to-all-start.1 = ((bf16[32,64,512]{2,1,0:T(8,128)(2,1)}), bf16[32,64,512]{2,1,0:T(8,128)(2,1)}, u32[]{:S(2)}, u32[]{:S(2)}) async-start(bf16[32,64,512]{2,1,0:T(8,128)(2,1)} %select_select_fusion), calls=%async_computation.1 | async-start | bytes 4194304 | tf_op jit(solution)/shard_map/all_to_all | solution.py:43
  427.5 77.9 %all-gather.2.cloned.1.call-done = f32[256,1024]{1,0:T(8,128)} async-done(((f32[8,1024]{1,0:T(8,128)}), f32[256,1024]{1,0:T(8,128)}) %all-gather.2.cloned.1.call-update) | async-done | bytes 1048592 | tf_op jit(solution)/shard_map/all_gather | solution.py:119
  505.4 1.0 slice_reduce_fusion
  506.4 0.7 iota_reduce_fusion
  507.1 0.5 compare_and_fusion.1
  507.7 2.1 slice.108
  509.8 2.3 gather_fusion.4
  512.1 0.9 copy.120
  513.0 0.8 copy.121
  513.8 1.0 broadcast_select_fusion.3
  514.8 0.8 log_add_fusion
  515.6 0.8 fusion.3
  516.4 1.0 copy-done
  517.3 0.8 fusion.5
  518.3 2.4 broadcast_in_dim.169
  520.7 2.5 scatter_fusion
  523.2 0.6 copy-done.25
  524.2 0.9 squeeze.45
  525.2 0.9 squeeze.44
  526.1 1.0 fusion.55
  527.4 0.3 reshape.637
  527.7 45.7 %psum.21 = f32[4,191]{1,0:T(4,128)S(1)} all-reduce(f32[4,191]{1,0:T(4,128)S(1)} %reduce_sum.58), channel_id=1, replica_groups=mesh['grp'=4,'seq'=32,'mp'=4] {'seq'}, use_global_device_ids=true, to_apply=%region_13.14 | all-reduce | flops 764 | bytes 6112 | tf_op jit(solution)/shard_map/psum | solution.py:184
  573.4 8.8 %psum.22 = f32[4,191]{1,0:T(4,128)S(1)} all-reduce(f32[4,191]{1,0:T(4,128)S(1)} %psum.21), channel_id=1, replica_groups=mesh['grp'=4,'seq'=32,'mp'=4] {'grp'}, use_global_device_ids=true, to_apply=%region_14.15 | all-reduce | flops 764 | bytes 6112 | tf_op jit(solution)/shard_map/psum | solution.py:184
  582.2 0.6 multiply_reduce_fusion.2
  582.8 1.2 copy_select_fusion.1
  584.0 9.1 %psum.23 = f32[]{:T(128)} all-reduce(f32[]{:T(128)} %multiply_reduce_fusion.2), channel_id=1, replica_groups=mesh['grp'=4,'seq'=32,'mp'=4] {'mp'}, use_global_device_ids=true, to_apply=%region_16.17 | all-reduce | flops 1 | bytes 8 | tf_op jit(solution)/shard_map/psum | solution.py:185
  593.1 0.7 iota_reduce_fusion.2
  593.8 1.7 gather_fusion.1
  595.6 0.4 gather.31
  596.0 0.6 broadcast_in_dim.155
  596.6 0.6 broadcast_in_dim.159
  597.2 0.3 fusion.13
  597.5 2.2 multiply_convert_fusion
  599.8 3.8 copy.129
  604.4 0.6 broadcast_multiply_fusion
  605.0 2.2 gather_fusion.3
  607.3 0.5 multiply_reduce_fusion.1
  608.1 5.7 collective-permute-start
  614.0 1.9 collective-permute-done
  615.9 17.8 %reduce-scatter.2.cloned.1.call-done = bf16[1,2,64,512]{3,2,1,0:T(8,128)(2,1)} async-done(((bf16[32,2,64,512]{3,2,1,0:T(8,128)(2,1)}), bf16[1,2,64,512]{3,2,1,0:T(8,128)(2,1)}) %reduce-scatter.2.cloned.1.call-update) | async-done | bytes 131088 | tf_op jit(solution)/shard_map/reduce_scatter | solution.py:179
  633.7 0.8 slice_bitcast_fusion.1
  634.5 3.6 collective-permute-start.1
  638.1 0.7 maximum_bitcast_fusion
  638.8 0.9 slice.121
  639.7 0.6 collective-permute-done.1
  640.3 0.7 maximum_bitcast_fusion.1
  (119 shorter events, 4.0 us)
Async XLA Ops:
  17.1 17.0 %copy-start.23 = (s32[1,8]{1,0:T(1,128)S(1)}, s32[1,8]{1,0:T(1,128)}, u32[]{:S(2)}) copy-start(s32[1,8]{1,0:T(1,128)} %param.9) | copy-start | bytes 100
  17.1 17.2 %copy-start.22 = (f32[4,191]{1,0:T(4,128)S(1)}, f32[4,191]{1,0:T(4,128)}, u32[]{:S(2)}) copy-start(f32[4,191]{1,0:T(4,128)} %param.10) | copy-start | bytes 9172
  17.1 377.5 %all-to-all-start = ((bf16[32,128,2,512]{3,2,1,0:T(2,128)(2,1)}), bf16[32,128,2,512]{3,2,1,0:T(2,128)(2,1)}, u32[]{:S(2)}, u32[]{:S(2)}) async-start(bf16[32,128,2,512]{3,2,1,0:T(2,128)(2,1)} %stack.21), calls=%async_computation | async-start | bytes 16777216 | tf_op jit(solution)/shard_map/all_to_all | solution.py:62
  34.1 1.6 copy-start.8
  34.1 471.3 %all-gather.2.cloned.1.call-start = ((), (), s32[]{:S(2)}) async-start(), calls=%async_computation.3 | async-start | bytes 1081344 | tf_op jit(solution)/shard_map/all_gather | solution.py:119
  34.2 5.4 copy-start.21
  39.5 3.5 copy-start.24
  39.6 362.0 %copy-start.15 = (pred[8,64]{1,0:T(8,128)(4,1)}, pred[8,64]{1,0:T(8,128)(4,1)S(1)}, u32[]{:S(2)}) copy-start(pred[8,64]{1,0:T(8,128)(4,1)S(1)} %get-tuple-element.50) | copy-start | bytes 1540
  39.7 363.4 %copy-start.17 = (pred[8,64]{1,0:T(8,128)(4,1)}, pred[8,64]{1,0:T(8,128)(4,1)S(1)}, u32[]{:S(2)}) copy-start(pred[8,64]{1,0:T(8,128)(4,1)S(1)} %get-tuple-element.51) | copy-start | bytes 1540
  401.3 1.7 copy-start.4
  401.6 2.2 copy-start.2
  406.3 1.8 copy-start.12
  406.3 1.8 copy-start.13
  414.5 190.5 %all-to-all-start.1 = ((bf16[32,64,512]{2,1,0:T(8,128)(2,1)}), bf16[32,64,512]{2,1,0:T(8,128)(2,1)}, u32[]{:S(2)}, u32[]{:S(2)}) async-start(bf16[32,64,512]{2,1,0:T(8,128)(2,1)} %select_select_fusion), calls=%async_computation.1 | async-start | bytes 4194304 | tf_op jit(solution)/shard_map/all_to_all | solution.py:43
  427.4 88.2 %copy-start.9 = (bf16[8,64,4,128]{3,2,1,0:T(4,128)(2,1)S(1)}, bf16[8,64,4,128]{3,2,1,0:T(4,128)(2,1)}, u32[]{:S(2)}) copy-start(bf16[8,64,4,128]{3,2,1,0:T(4,128)(2,1)} %get-tuple-element.35) | copy-start | bytes 1572868
  427.4 206.3 %reduce-scatter.2.cloned.1.call-start = ((), (), s32[]{:S(2)}) async-start(), calls=%async_computation.4 | async-start | bytes 4325376 | tf_op jit(solution)/shard_map/reduce_scatter | solution.py:179
  506.4 3.4 copy-start.19
  513.8 3.5 copy-start.3
  515.6 2.6 copy-start.10
  516.4 1.0 copy-start
  518.3 2.4 copy-start.14
  523.2 0.7 copy-start.25
  523.2 1.0 copy-start.5
  523.2 2.9 copy-start.1
  525.2 57.6 %copy-start.6 = (bf16[8,1,64,4,128]{4,3,2,0,1:T(4,128)(2,1)S(1)}, bf16[8,1,64,4,128]{4,3,2,0,1:T(4,128)(2,1)}, u32[]{:S(2)}) copy-start(bf16[8,1,64,4,128]{4,3,2,0,1:T(4,128)(2,1)} %squeeze.45) | copy-start | bytes 1572868
  525.2 57.6 %copy-start.16 = (pred[8,64]{1,0:T(8,128)(4,1)S(1)}, pred[8,64]{1,0:T(8,128)(4,1)}, u32[]{:S(2)}) copy-start(pred[8,64]{1,0:T(8,128)(4,1)} %copy-done.15) | copy-start | bytes 1540
  525.2 57.6 %copy-start.18 = (pred[8,64]{1,0:T(8,128)(4,1)S(1)}, pred[8,64]{1,0:T(8,128)(4,1)}, u32[]{:S(2)}) copy-start(pred[8,64]{1,0:T(8,128)(4,1)} %copy-done.17) | copy-start | bytes 1540
  526.1 56.7 %copy-start.7 = (bf16[8,1,64,4,128]{4,3,2,0,1:T(4,128)(2,1)S(1)}, bf16[8,1,64,4,128]{4,3,2,0,1:T(4,128)(2,1)}, u32[]{:S(2)}) copy-start(bf16[8,1,64,4,128]{4,3,2,0,1:T(4,128)(2,1)} %squeeze.44) | copy-start | bytes 1572868
  527.1 66.1 %copy-start.20 = (f32[256]{0:T(256)S(1)}, f32[256]{0:T(256)}, u32[]{:S(2)}) copy-start(f32[256]{0:T(256)} %copy-done.19) | copy-start | bytes 3076
  527.2 70.0 %copy-start.11 = (f32[8,64,4]{1,2,0:T(4,128)S(1)}, f32[8,64,4]{1,2,0:T(4,128)}, u32[]{:S(2)}) copy-start(f32[8,64,4]{1,2,0:T(4,128)} %copy-done.10) | copy-start | bytes 24580
  599.7 4.5 copy-start.27
  603.6 3.7 copy-start.26
  608.1 7.7 %collective-permute-start = (bf16[64,512]{1,0:T(8,128)(2,1)S(1)}, bf16[64,512]{1,0:T(8,128)(2,1)S(1)}, u32[]{:S(2)}, u32[]{:S(2)}) collective-permute-start(bf16[64,512]{1,0:T(8,128)(2,1)S(1)} %bitcast.180), channel_id=1, source_target_pairs={{0,4},{4,8},{8,12},{12,16},{16,20},{20,24},{24,28},{28,32},{32,36}... | collective-permute-start | bytes 196616 | tf_op jit(solution)/shard_map/ppermute | solution.py:14
  634.5 5.7 collective-permute-start.1
Sparse Core Ops, SparseCore 0:
  407.5 97.8 all-gather.1
  523.3 110.3 reduce-scatter.1
